TPU v7x, 32 devices: a whole 2x2x4 slice. The times are simulated.
32 devices in a mesh: seq: 8 (over y, x, core), head: 4 (over z).
Axes of the slice: x: 2, y: 2, z: 4, core: 2. Of those that a mesh axis runs over, the one named last changes fastest.
Arguments:
- tokens: bfloat16 [4096, 5376], P('seq', 'head'), may hold values from -32 to 32
- query_weight: bfloat16 [5376, 4096], P(None, 'head'), may hold values from -1 to 1
- key_weight: bfloat16 [5376, 2048], P(None, 'head'), may hold values from -1 to 1
- value_weight: bfloat16 [5376, 2048], P(None, 'head'), may hold values from -0.078125 to 0.078125
- output_grad: bfloat16 [4096, 4096], P('seq', 'head'), may hold values from -48 to 48
- segments: int32 [4096], replicated, may hold values from 0 to 3, never falling along the last dimension, each value on 1 to 2048 neighbouring positions
Outputs:
- token_grad: bfloat16 [4096, 5376], P('seq', 'head')
- query_weight_grad: bfloat16 [5376, 4096], P('seq', 'head')
- key_weight_grad: bfloat16 [5376, 2048], P('seq', 'head')
- value_weight_grad: bfloat16 [5376, 2048], P('seq', 'head')
Inputs may be any that keep to these rules, and one draw needn't show every extreme that they name: `segments`: segment numbers never fall along the tokens; a segment has at most 2048 tokens.
All inputs are finite; a program needn't handle non-finite values.
Results may differ from a plain program's by a relative error of at most 0.015.
The roundings to bfloat16 on the way count: a program that leaves them out, or rounds other values in their place, can miss the bound.
Values may be sent and summed in bfloat16 or wider, within the bound.
No kernel may reach another device: no remote copies, remote signals or barrier semaphores. Data moves between devices by JAX's collectives and lax.ppermute only.
A program may use at most 192 MiB of HBM per device.

v0:
```python
import jax
import jax.numpy as jnp
from jax import lax
from jax.sharding import PartitionSpec as P

D = 5376
HEADS = 32
KV_HEADS = 16
HEAD_DIM = 128
WINDOW = 1024
HOPS = 2
neg_large = -1e30


def passed_along(x, axis, by):
    count = lax.axis_size(axis)
    pairs = [(i, i + by) for i in range(count) if 0 <= i + by < count]
    return lax.ppermute(x, axis, pairs)


def contract_last(left, right):
    return lax.dot_general(
        left, right, (((1,), (1,)), ((), ())), preferred_element_type=jnp.float32
    )


def contract_first(left, right):
    return lax.dot_general(
        left, right, (((0,), (0,)), ((), ())), preferred_element_type=jnp.float32
    )


def attend(queries, key_value, grads, query_first, key_first, seg_query, seg_key):
    tok_rows = queries.shape[0]
    key_rows = key_value.shape[1]
    groups = HEADS // KV_HEADS
    kv_local = key_value.shape[2] // HEAD_DIM
    score_scale = (D / HEADS) ** (-0.5)
    query_four = queries.reshape(tok_rows, kv_local, groups, HEAD_DIM)
    grad_four = grads.reshape(tok_rows, kv_local, groups, HEAD_DIM)
    key_three = key_value[0].reshape(key_rows, kv_local, HEAD_DIM)
    value_three = key_value[1].reshape(key_rows, kv_local, HEAD_DIM)
    query_pos = query_first + jnp.arange(tok_rows, dtype=jnp.int32)
    key_pos = key_first + jnp.arange(key_rows, dtype=jnp.int32)
    spacing = query_pos[:, None] - key_pos[None, :]
    allowed = (
        (key_pos >= 0)[None, :]
        & (spacing >= 0)
        & (spacing < WINDOW)
        & (seg_query[:, None] == seg_key[None, :])
    )
    scores = (
        jnp.einsum("akgd,ckd->kgac", query_four, key_three, preferred_element_type=jnp.float32)
        * score_scale
    )
    masked = jnp.where(allowed, scores, neg_large)
    row_max = jnp.max(masked, axis=-1, keepdims=True)
    expo = jnp.where(allowed, jnp.exp(masked - row_max), 0.0)
    probs = expo / jnp.sum(expo, axis=-1, keepdims=True)
    dprobs = jnp.einsum(
        "akgd,ckd->kgac", grad_four, value_three, preferred_element_type=jnp.float32
    )
    center = jnp.sum(probs * dprobs, axis=-1, keepdims=True)
    dscores = (probs * (dprobs - center)).astype(jnp.bfloat16)
    probs_low = probs.astype(jnp.bfloat16)
    query_grad = (
        (
            jnp.einsum("kgac,ckd->akgd", dscores, key_three, preferred_element_type=jnp.float32)
            * score_scale
        )
        .reshape(tok_rows, -1)
        .astype(jnp.bfloat16)
    )
    key_grad = (
        jnp.einsum("kgac,akgd->ckd", dscores, query_four, preferred_element_type=jnp.float32)
        * score_scale
    ).reshape(key_rows, -1)
    value_grad = jnp.einsum(
        "kgac,akgd->ckd", probs_low, grad_four, preferred_element_type=jnp.float32
    ).reshape(key_rows, -1)
    return (query_grad, jnp.stack([key_grad, value_grad]))


def per_device(tokens, query_weight, key_weight, value_weight, output_grad, segments):
    tok_rows = tokens.shape[0]
    hop_count = HOPS
    margin = hop_count * tok_rows
    gathered = lax.all_gather(tokens, "head", axis=1, tiled=True)
    queries = jnp.dot(gathered, query_weight, preferred_element_type=jnp.float32).astype(
        jnp.bfloat16
    )
    keys_own = jnp.dot(gathered, key_weight, preferred_element_type=jnp.float32).astype(
        jnp.bfloat16
    )
    values_own = jnp.dot(gathered, value_weight, preferred_element_type=jnp.float32).astype(
        jnp.bfloat16
    )
    key_value = jnp.stack([keys_own, values_own])
    blocks = [key_value] * (hop_count + 1)
    moving = key_value
    for distance in range(1, hop_count + 1):
        moving = passed_along(moving, "seq", 1)
        blocks[hop_count - distance] = moving
    keys_all = jnp.concatenate(blocks, axis=1)
    position = lax.axis_index("seq")
    query_first = position * tok_rows
    seg_query = lax.dynamic_slice_in_dim(segments, query_first, tok_rows, 0)
    seg_padded = jnp.concatenate([jnp.full((margin,), -1, jnp.int32), segments], axis=0)
    seg_key = lax.dynamic_slice_in_dim(seg_padded, query_first, (hop_count + 1) * tok_rows, 0)
    query_grad, kv_grad = attend(
        queries, keys_all, output_grad, query_first, query_first - margin, seg_query, seg_key
    )
    pieces = [
        kv_grad[:, block * tok_rows : (block + 1) * tok_rows] for block in range(hop_count + 1)
    ]
    carried = pieces[0]
    for distance in range(1, hop_count + 1):
        carried = pieces[distance] + passed_along(carried.astype(jnp.bfloat16), "seq", -1).astype(
            carried.dtype
        )
    key_grad = carried[0].astype(jnp.bfloat16)
    value_grad = carried[1].astype(jnp.bfloat16)
    partial_term = (
        contract_last(query_grad, query_weight)
        + contract_last(key_grad, key_weight)
        + contract_last(value_grad, value_weight)
    )
    token_grad = lax.psum_scatter(
        partial_term.astype(jnp.bfloat16), "head", scatter_dimension=1, tiled=True
    )
    proj_grads = jnp.concatenate([query_grad, key_grad, value_grad], axis=1)
    summed = lax.psum_scatter(
        contract_first(gathered, proj_grads).astype(jnp.bfloat16),
        "seq",
        scatter_dimension=0,
        tiled=True,
    ).astype(jnp.float32)
    summed = summed * (tok_rows * lax.axis_size("seq")) ** (-0.5)
    q_width = query_weight.shape[1]
    k_width = key_weight.shape[1]
    query_weight_grad = summed[:, :q_width].astype(jnp.bfloat16)
    key_weight_grad = summed[:, q_width : q_width + k_width].astype(jnp.bfloat16)
    value_weight_grad = summed[:, q_width + k_width :].astype(jnp.bfloat16)
    return (token_grad, query_weight_grad, key_weight_grad, value_weight_grad)


def solution(mesh):
    in_specs = (
        P("seq", "head"),
        P(None, "head"),
        P(None, "head"),
        P(None, "head"),
        P("seq", "head"),
        P(),
    )
    out_specs = (P("seq", "head"), P("seq", "head"), P("seq", "head"), P("seq", "head"))
    return jax.shard_map(
        per_device, mesh=mesh, in_specs=in_specs, out_specs=out_specs, check_vma=False
    )
```

profile of v0, /device:TPU:0, one launch (start us, length us, event | category | flops | bytes accessed | tf_op | source)
XLA Modules:
  0.0 569.0 jit_solution(12160398720478876539)
XLA Ops:
  7.2 0.7 all-gather.2.cloned.1.call-update
  7.9 0.0 reduce-scatter.7.cloned.1.call-start
  7.9 106.7 %all-gather.2.cloned.1.call-done = bf16[512,5376]{0,1:T(8,128)(2,1)} async-done(((bf16[512,1344]{0,1:T(8,128)(2,1)}), bf16[512,5376]{0,1:T(8,128)(2,1)}) %all-gather.2.cloned.1.call-update) | async-done | bytes 5505040 | tf_op jit(solution)/shard_map/all_gather | solution.py:88
  114.7 7.3 %fusion.32 = bf16[1,512,512]{2,1,0:T(8,128)(2,1)S(1)} fusion(bf16[512,5376]{0,1:T(8,128)(2,1)} %all-gather.2.cloned.1.call-done, bf16[5376,512]{1,0:T(8,128)(2,1)} %param.9), kind=kOutput, calls=%fused_computation.52 | convolution fusion | flops 2818834432 | bytes 11534336 | tf_op jit(solution)/shard_map/dot_general | solution.py:95
  122.1 5.7 fusion.31
  127.8 0.1 pad_maximum_fusion.1
  127.9 2.9 collective-permute-start
  130.8 1.3 copy.53
  132.1 0.1 dynamic_slice.6
  132.2 0.1 pad_dynamic-slice_fusion
  132.3 2.6 fusion.16
  134.9 10.3 %collective-permute-start.1 = (bf16[2,512,512]{2,1,0:T(8,128)(2,1)}, bf16[2,512,512]{2,1,0:T(8,128)(2,1)S(1)}, u32[]{:S(2)}, u32[]{:S(2)}) collective-permute-start(bf16[2,512,512]{2,1,0:T(8,128)(2,1)} %collective-permute-done), channel_id=1, source_target_pairs={{0,4},{4,8},{8,12},{12,16},{16,20},{20,24},{24,28},{1,5},{5,9},{9,... | collective-permute-start | bytes 3145736 | tf_op jit(solution)/shard_map/ppermute | solution.py:18
  145.2 10.4 %convolution_convert_fusion.1 = bf16[512,1024]{1,0:T(8,128)(2,1)S(1)} fusion(bf16[512,5376]{0,1:T(8,128)(2,1)} %all-gather.2.cloned.1.call-done, bf16[5376,1024]{1,0:T(8,128)(2,1)} %param.7), kind=kOutput, calls=%fused_computation.48 | convolution fusion | flops 5637668864 | bytes 17563648 | tf_op jit(solution)/shard_map/dot_general | solution.py:89
  155.6 1.3 copy.52
  156.9 1.4 maximum_maximum_fusion
  158.3 1.4 fusion.38
  159.7 0.4 reshape_squeeze.6
  160.1 1.0 copy.38
  161.1 2.8 reshape_squeeze.7
  163.9 17.4 %fusion.39 = (f32[4,2,512]{2,1,0:T(2,128)S(1)}, f32[4,2,512,1536]{2,3,1,0:T(8,128)}) fusion(pred[512,1536]{0,1:T(8,128)(4,1)} %fusion.16, bf16[1536,4,128,1]{0,2,3,1:T(8,128)(2,1)S(1)} %copy.38, bf16[512,4,2,128]{0,3,2,1:T(8,128)(2,1)} %bitcast.77), kind=kOutput, calls=%fused_computation.66 | convolution fusion | flops 1642071552 | bytes 28590080 | tf_op jit(solution)/shard_map/sub | solution.py:58
  181.3 12.5 %fusion.6 = f32[4,1536,128,1]{1,2,3,0:T(8,128)} fusion(bf16[512,4,2,128]{0,3,2,1:T(8,128)(2,1)} %bitcast.80, f32[4,2,512,1536]{2,3,1,0:T(8,128)} %get-tuple-element.19, f32[4,2,512]{2,1,0:T(2,128)S(1)} %get-tuple-element.18), kind=kOutput, calls=%fused_computation.11 | convolution fusion | flops 1623195648 | bytes 29376512 | tf_op jit(solution)/shard_map/kgac,akgd->ckd/dot_general | solution.py:78
  193.8 16.6 %fusion.1 = (f32[4,2,512]{2,1,0:T(2,128)S(1)}, f32[4,1536,512,2]{2,1,3,0:T(8,128)}) fusion(f32[4,2,512,1536]{2,3,1,0:T(8,128)} %get-tuple-element.19, f32[4,2,512]{2,1,0:T(2,128)S(1)} %get-tuple-element.18, bf16[512,4,2,128]{0,3,2,1:T(8,128)(2,1)S(1)} %bitcast.81, bf16[1536,4,128,1]{2,1,0,3:T(4,128)(2,1)S(1)} %bitcast.79), kind=kOutput, calls=%fused_computation.3 | convolution fusion | flops 1629483008 | bytes 52985856 | tf_op jit(solution)/shard_map/akgd,ckd->kgac/dot_general | solution.py:60
  210.4 16.8 %fusion.3 = bf16[4,2,512,1536]{2,3,1,0:T(8,128)(2,1)S(1)} fusion(f32[4,1536,512,2]{2,1,3,0:T(8,128)} %get-tuple-element.21, f32[4,2,512]{2,1,0:T(2,128)S(1)} %get-tuple-element.20, f32[4,2,512,1536]{2,3,1,0:T(8,128)} %get-tuple-element.19, f32[4,2,512]{2,1,0:T(2,128)S(1)} %get-tuple-element.18), kind=kLoop, calls=%fused_computation.5 | loop fusion | flops 25165824 | bytes 62947328 | tf_op jit(solution)/shard_map/convert_element_type | solution.py:64
  227.2 7.0 %fusion.13 = f32[4,128,1536]{2,1,0:T(8,128)} fusion(bf16[512,4,2,128]{0,3,2,1:T(8,128)(2,1)} %bitcast.78, bf16[4,2,512,1536]{2,3,1,0:T(8,128)(2,1)S(1)} %fusion.3), kind=kOutput, calls=%fused_computation.27 | convolution fusion | flops 1611399168 | bytes 16777216 | tf_op jit(solution)/shard_map/kgac,akgd->ckd/dot_general | solution.py:75
  234.2 1.8 fusion.23
  236.1 1.6 collective-permute-start.2
  237.7 5.4 collective-permute-done.2
  243.1 0.4 fusion.19
  243.5 1.3 collective-permute-start.3
  244.8 2.8 multiply_convert_fusion.1
  247.6 12.7 %collective-permute-done.3 = bf16[2,512,512]{1,2,0:T(8,128)(2,1)S(1)} collective-permute-done((bf16[2,512,512]{1,2,0:T(8,128)(2,1)S(1)}, bf16[2,512,512]{1,2,0:T(8,128)(2,1)S(1)}, u32[]{:S(2)}, u32[]{:S(2)}) %collective-permute-start.3) | collective-permute-done | bytes 1048608 | tf_op jit(solution)/shard_map/ppermute | solution.py:18
  260.2 0.4 fusion.22
  260.6 0.1 slice_bitcast_fusion.1
  260.7 20.0 %fusion.5 = bf16[5376,2048]{0,1:T(8,128)(2,1)} fusion(bf16[512,5376]{0,1:T(8,128)(2,1)} %all-gather.2.cloned.1.call-done, bf16[512,512]{0,1:T(8,128)(2,1)S(1)} %get-tuple-element.17, bf16[512,512]{0,1:T(8,128)(2,1)S(1)} %get-tuple-element.16, bf16[512,1024]{0,1:T(8,128)(2,1)S(1)} %bitcast.82), kind=kOutput, calls=%fused_computation.10 | convolution fusion | flops 11291590656 | bytes 29622272 | tf_op jit(solution)/shard_map/dot_general | solution.py:28
  280.7 28.2 %copy.50 = bf16[5376,2048]{1,0:T(8,128)(2,1)} copy(bf16[5376,2048]{0,1:T(8,128)(2,1)} %fusion.5) | data formatting | bytes 44040192
  308.9 0.0 reduce-scatter.5.cloned.1.call-start
  309.0 13.0 %fusion.40 = f32[512,5376]{0,1:T(8,128)} fusion(bf16[5376,1024]{1,0:T(8,128)(2,1)} %param.7, bf16[512,1024]{0,1:T(8,128)(2,1)S(1)} %bitcast.83), kind=kOutput, calls=%fused_computation.67 | convolution fusion | flops 5637144576 | bytes 23068672 | tf_op jit(solution)/shard_map/dot_general | solution.py:22
  321.9 9.3 %fusion.36 = f32[512,5376]{0,1:T(8,128)} fusion(bf16[5376,512]{1,0:T(8,128)(2,1)} %param.8, bf16[2,512,512]{1,2,0:T(8,128)(2,1)S(1)} %fusion.22), kind=kOutput, calls=%fused_computation.63 | convolution fusion | flops 2818572288 | bytes 17039360 | tf_op jit(solution)/shard_map/dot_general | solution.py:22
  331.3 19.3 %add_convert_fusion = bf16[512,5376]{0,1:T(8,128)(2,1)} fusion(f32[512,5376]{0,1:T(8,128)} %fusion.40, f32[512,5376]{0,1:T(8,128)} %fusion.36, bf16[5376,512]{1,0:T(8,128)(2,1)} %param.9, bf16[2,512,512]{1,2,0:T(8,128)(2,1)S(1)} %fusion.22), kind=kOutput, calls=%fused_computation.17 | convolution fusion | flops 2826829824 | bytes 33554432 | tf_op jit(solution)/shard_map/dot_general | solution.py:22
  350.6 111.0 %reduce-scatter.7.cloned.1.call-done = bf16[672,2048]{1,0:T(8,128)(2,1)} async-done(((bf16[5376,2048]{1,0:T(8,128)(2,1)}), bf16[672,2048]{1,0:T(8,128)(2,1)}) %reduce-scatter.7.cloned.1.call-update) | async-done | bytes 2752528
  461.6 4.6 copy.51
  466.2 2.5 multiply_convert_fusion
  468.7 1.3 slice.54
  469.9 2.9 copy.33
  472.9 1.3 fusion.37
  474.1 2.2 copy.34
  476.4 2.2 copy.35
  478.6 83.9 %reduce-scatter.5.cloned.1.call-done = bf16[512,1344]{0,1:T(8,128)(2,1)} async-done(((bf16[512,5376]{0,1:T(8,128)(2,1)}), bf16[512,1344]{0,1:T(8,128)(2,1)}) %reduce-scatter.5.cloned.1.call-update) | async-done | bytes 1376272 | tf_op jit(solution)/shard_map/reduce_scatter | solution.py:128
  (25 shorter events, 0.1 us)
Async XLA Ops:
  7.2 107.5 %all-gather.2.cloned.1.call-start = ((), (), s32[]{:S(2)}) async-start(), calls=%async_computation.2 | async-start | bytes 6881280 | tf_op jit(solution)/shard_map/all_gather | solution.py:88
  7.9 453.7 %reduce-scatter.7.cloned.1.call-start = ((), (), s32[]{:S(2)}) async-start(), calls=%async_computation.4 | async-start | bytes 24772608
  114.7 7.4 %copy-start.8 = (bf16[512,5376]{0,1:T(8,128)(2,1)S(1)}, bf16[512,5376]{0,1:T(8,128)(2,1)}, u32[]{:S(2)}) copy-start(bf16[512,5376]{0,1:T(8,128)(2,1)} %all-gather.2.cloned.1.call-done) | copy-start | bytes 16515076
  122.1 8.7 %copy-start.4 = (bf16[512,1024]{1,0:T(8,128)(2,1)S(1)}, bf16[512,1024]{1,0:T(8,128)(2,1)}, u32[]{:S(2)}) copy-start(bf16[512,1024]{1,0:T(8,128)(2,1)} %param.10) | copy-start | bytes 3145732
  122.1 10.0 %copy-start.7 = (s32[4096]{0:T(1024)S(1)}, s32[4096]{0:T(1024)}, u32[]{:S(2)}) copy-start(s32[4096]{0:T(1024)} %param.11) | copy-start | bytes 49156
  127.9 7.0 %collective-permute-start = (bf16[2,512,512]{2,1,0:T(8,128)(2,1)S(1)}, bf16[2,512,512]{2,1,0:T(8,128)(2,1)}, u32[]{:S(2)}, u32[]{:S(2)}) collective-permute-start(bf16[2,512,512]{2,1,0:T(8,128)(2,1)S(1)} %pad_maximum_fusion.1), channel_id=1, source_target_pairs={{0,4},{4,8},{8,12},{12,16},{16,20},{20,24},{24,28},{1,5},{5,9},{9,... | collective-permute-start | bytes 3145736 | tf_op jit(solution)/shard_map/ppermute | solution.py:18
  134.9 22.0 %collective-permute-start.1 = (bf16[2,512,512]{2,1,0:T(8,128)(2,1)}, bf16[2,512,512]{2,1,0:T(8,128)(2,1)S(1)}, u32[]{:S(2)}, u32[]{:S(2)}) collective-permute-start(bf16[2,512,512]{2,1,0:T(8,128)(2,1)} %collective-permute-done), channel_id=1, source_target_pairs={{0,4},{4,8},{8,12},{12,16},{16,20},{20,24},{24,28},{1,5},{5,9},{9,... | collective-permute-start | bytes 3145736 | tf_op jit(solution)/shard_map/ppermute | solution.py:18
  161.1 20.2 %copy-start.2 = (bf16[1536,4,128,1]{0,2,3,1:T(8,128)(2,1)}, bf16[1536,4,128,1]{0,2,3,1:T(8,128)(2,1)S(1)}, u32[]{:S(2)}) copy-start(bf16[1536,4,128,1]{0,2,3,1:T(8,128)(2,1)S(1)} %copy.38) | copy-start | bytes 4718596
  181.3 12.5 %copy-start.5 = (bf16[512,1024]{0,1:T(8,128)(2,1)S(1)}, bf16[512,1024]{0,1:T(8,128)(2,1)}, u32[]{:S(2)}) copy-start(bf16[512,1024]{0,1:T(8,128)(2,1)} %copy.53) | copy-start | bytes 3145732
  234.2 8.9 %copy-start = (f32[4,128,1536]{2,1,0:T(8,128)S(1)}, f32[4,128,1536]{2,1,0:T(8,128)}, u32[]{:S(2)}) copy-start(f32[4,128,1536]{2,1,0:T(8,128)} %fusion.13) | copy-start | bytes 9437188
  234.2 8.9 %copy-start.1 = (f32[4,1536,128,1]{1,2,3,0:T(8,128)S(1)}, f32[4,1536,128,1]{1,2,3,0:T(8,128)}, u32[]{:S(2)}) copy-start(f32[4,1536,128,1]{1,2,3,0:T(8,128)} %fusion.6) | copy-start | bytes 9437188
  236.1 8.7 %copy-start.3 = (bf16[1536,4,128,1]{0,2,3,1:T(8,128)(2,1)S(1)}, bf16[1536,4,128,1]{0,2,3,1:T(8,128)(2,1)}, u32[]{:S(2)}) copy-start(bf16[1536,4,128,1]{0,2,3,1:T(8,128)(2,1)} %copy-done.2) | copy-start | bytes 4718596
  236.1 7.0 %collective-permute-start.2 = (bf16[2,512,512]{1,2,0:T(8,128)(2,1)S(1)}, bf16[2,512,512]{1,2,0:T(8,128)(2,1)S(1)}, u32[]{:S(2)}, u32[]{:S(2)}) collective-permute-start(bf16[2,512,512]{1,2,0:T(8,128)(2,1)S(1)} %fusion.23), channel_id=1, source_target_pairs={{4,0},{8,4},{12,8},{16,12},{20,16},{24,20},{28,24},{5,1},{9,5},{13... | collective-permute-start | bytes 3145736 | tf_op jit(solution)/shard_map/ppermute | solution.py:18
  243.5 16.8 %collective-permute-start.3 = (bf16[2,512,512]{1,2,0:T(8,128)(2,1)S(1)}, bf16[2,512,512]{1,2,0:T(8,128)(2,1)S(1)}, u32[]{:S(2)}, u32[]{:S(2)}) collective-permute-start(bf16[2,512,512]{1,2,0:T(8,128)(2,1)S(1)} %fusion.19), channel_id=1, source_target_pairs={{4,0},{8,4},{12,8},{16,12},{20,16},{24,20},{28,24},{5,1},{9,5},{13... | collective-permute-start | bytes 3145736 | tf_op jit(solution)/shard_map/ppermute | solution.py:18
  247.6 13.1 %copy-start.6 = (bf16[4,128,2,512]{3,1,2,0:T(8,128)(2,1)S(1)}, bf16[4,128,2,512]{3,1,2,0:T(8,128)(2,1)}, u32[]{:S(2)}) copy-start(bf16[4,128,2,512]{3,1,2,0:T(8,128)(2,1)} %multiply_convert_fusion.1) | copy-start | bytes 3145732
  308.9 253.6 %reduce-scatter.5.cloned.1.call-start = ((), (), s32[]{:S(2)}) async-start(), calls=%async_computation.3 | async-start | bytes 6881280 | tf_op jit(solution)/shard_map/reduce_scatter | solution.py:128
Sparse Core Ops, SparseCore 0:
  9.6 105.0 all-gather.1
  309.0 152.5 reduce-scatter.6
  464.5 97.9 reduce-scatter.4
where the time goes:
time: 570 us; the launch traced here: 569 us
  waiting for transfers between devices  320 us (56%)
  matrix products  141 us (25%)
  local copies, waits for them, and re-layouts  51.1 us (9%)
  other arithmetic  26 us (5%)
  starting transfers between devices  16.2 us (3%)
  between operations  14 us (2%)
    unnamed x4, waiting for transfers between devices  112 us
    all_gather x1, waiting for transfers between devices, per_device(): gathered = lax.all_gather(tokens, 'head', axis=1, tiled=True)  107 us
    reduce_scatter x1, waiting for transfers between devices, per_device(): lax.psum_scatter(partial_term.astype(jnp.bfloat16), 'head', scatter_dimen...  83.9 us
    dot_general x3, matrix products, contract_last(): lax.dot_general(left, right, (((1,), (1,)), ((), ())), preferred_element_...  41.6 us
    unnamed x23, local copies, waits for them, and re-layouts  40.2 us
    dot_general x1, matrix products, contract_first(): lax.dot_general(left, right, (((0,), (0,)), ((), ())), preferred_element_...  20 us
    ppermute x4, waiting for transfers between devices, passed_along(): return lax.ppermute(x, axis, pairs)  18.1 us
    sub x1, matrix products, attend(): expo = jnp.where(allowed, jnp.exp(masked - row_max), 0.0)  17.4 us
  transfers between devices with their start and end apart: 7, of which 5 were waited for; matrix products, arithmetic and copies ran while one was open for 14% of the time, Pallas kernels for 0%

commit v1 on v0

--- a/solution.py
+++ b/solution.py
@@ -10,6 +10,22 @@
 WINDOW = 1024
 HOPS = 2
 neg_large = -1e30
+
+
+def detail_vectors(mesh_dim, w_in):
+    chunks = [w_in]
+    n_shards = lax.axis_size(mesh_dim)
+    for p in range(n_shards - 1):
+        chunks.append(
+            lax.ppermute(
+                chunks[-1],
+                axis_name=mesh_dim,
+                perm=[(i0, (i0 + 1) % n_shards) for i0 in range(n_shards)],
+            )
+        )
+    known = jnp.concatenate(chunks[::-1], 1)
+    parts_out = jnp.roll(known, (lax.axis_index(mesh_dim) + 1) * w_in.shape[1], 1)
+    return parts_out
 
 
 def passed_along(x, axis, by):
@@ -85,7 +101,7 @@
     tok_rows = tokens.shape[0]
     hop_count = HOPS
     margin = hop_count * tok_rows
-    gathered = lax.all_gather(tokens, "head", axis=1, tiled=True)
+    gathered = detail_vectors("head", tokens)
     queries = jnp.dot(gathered, query_weight, preferred_element_type=jnp.float32).astype(
         jnp.bfloat16
     )

time: 570 us -> 544 us (0.954)
  local copies, waits for them, and re-layouts: 51.1 us -> 19.8 us
    unnamed x4 -> x2, waiting for transfers between devices: 112 us -> 0.03 us
    reduce_scatter x0 -> x1, waiting for transfers between devices: none -> 111 us  [per_device(): lax.psum_scatter(contract_first(gathered, proj_grads).astype(jnp.bfloat16...]
    all_gather x1 -> x0, waiting for transfers between devices: 107 us -> none  [per_device(): gathered = lax.all_gather(tokens, 'head', axis=1, tiled=True)]
    ppermute x0 -> x3, waiting for transfers between devices: none -> 98.2 us  [detail_vectors(): lax.ppermute(chunks[-1], axis_name=mesh_dim, perm=[(i0, (i0 + 1) % n_shar...]
    unnamed x23 -> x35, local copies, waits for them, and re-layouts: 40.2 us -> 8.93 us
    reduce_scatter x1, waiting for transfers between devices: 83.9 us -> 96.1 us  [per_device(): lax.psum_scatter(partial_term.astype(jnp.bfloat16), 'head', scatter_dimen...]
  transfers between devices with their start and end apart: 7 -> 9, of which waited for: 5 -> 7; matrix products, arithmetic and copies ran while one was open for 14% -> 12% of each run, Pallas kernels for 0% -> 0%
where the time goes in v1:
time: 544 us; the launch traced here: 537 us
  waiting for transfers between devices  323 us (59%)
  matrix products  136 us (25%)
  other arithmetic  25.9 us (5%)
  local copies, waits for them, and re-layouts  19.8 us (4%)
  starting transfers between devices  19.1 us (4%)
  between operations  14.6 us (3%)
    reduce_scatter x1, waiting for transfers between devices, per_device(): lax.psum_scatter(contract_first(gathered, proj_grads).astype(jnp.bfloat16...  111 us
    ppermute x3, waiting for transfers between devices, detail_vectors(): lax.ppermute(chunks[-1], axis_name=mesh_dim, perm=[(i0, (i0 + 1) % n_shar...  98.2 us
    reduce_scatter x1, waiting for transfers between devices, per_device(): lax.psum_scatter(partial_term.astype(jnp.bfloat16), 'head', scatter_dimen...  96.1 us
    dot_general x3, matrix products, contract_last(): lax.dot_general(left, right, (((1,), (1,)), ((), ())), preferred_element_...  41.6 us
    dot_general x1, matrix products, contract_first(): lax.dot_general(left, right, (((0,), (0,)), ((), ())), preferred_element_...  20.3 us
    sub x1, matrix products, attend(): expo = jnp.where(allowed, jnp.exp(masked - row_max), 0.0)  17.5 us
    ppermute x4, waiting for transfers between devices, passed_along(): return lax.ppermute(x, axis, pairs)  17.3 us
    convert_element_type x1, other arithmetic, attend(): dscores = (probs * (dprobs - center)).astype(jnp.bfloat16)  16.8 us
  transfers between devices with their start and end apart: 9, of which 7 were waited for; matrix products, arithmetic and copies ran while one was open for 12% of the time, Pallas kernels for 0%

profile of v1, /device:TPU:0, one launch (start us, length us, event | category | flops | bytes accessed | tf_op | source)
XLA Modules:
  0.0 537.4 jit_solution(17517577569129410471)
XLA Ops:
  7.2 3.1 collective-permute-start
  10.3 32.4 %collective-permute-done = bf16[512,1344]{0,1:T(8,128)(2,1)S(1)} collective-permute-done((bf16[512,1344]{0,1:T(8,128)(2,1)}, bf16[512,1344]{0,1:T(8,128)(2,1)S(1)}, u32[]{:S(2)}, u32[]{:S(2)}) %collective-permute-start) | collective-permute-done | bytes 1376288 | tf_op jit(solution)/shard_map/ppermute | solution.py:20
  42.7 33.3 %collective-permute-done.1 = bf16[512,1344]{0,1:T(8,128)(2,1)} collective-permute-done((bf16[512,1344]{0,1:T(8,128)(2,1)S(1)}, bf16[512,1344]{0,1:T(8,128)(2,1)}, u32[]{:S(2)}, u32[]{:S(2)}) %collective-permute-start.1) | collective-permute-done | bytes 1376288 | tf_op jit(solution)/shard_map/ppermute | solution.py:20
  76.0 32.6 %collective-permute-done.2 = bf16[512,1344]{0,1:T(8,128)(2,1)} collective-permute-done((bf16[512,1344]{0,1:T(8,128)(2,1)}, bf16[512,1344]{0,1:T(8,128)(2,1)}, u32[]{:S(2)}, u32[]{:S(2)}) %collective-permute-start.2) | collective-permute-done | bytes 1376288 | tf_op jit(solution)/shard_map/ppermute | solution.py:20
  108.5 1.4 constant_dynamic-update-slice_fusion.7
  110.0 1.4 constant_dynamic-update-slice_fusion.6
  111.5 0.1 constant_dynamic-update-slice_fusion.4
  111.6 1.6 constant_dynamic-update-slice_fusion.3
  113.2 1.5 constant_dynamic-update-slice_fusion.2
  115.0 0.2 slice-done.1
  115.2 3.0 fusion.46
  118.2 2.2 copy-done.8
  120.4 0.3 slice-done.3
  120.7 3.0 fusion.49
  123.7 0.1 pad_maximum_fusion.1
  123.8 2.3 collective-permute-start.3
  126.1 1.3 copy.35
  127.6 2.6 fusion.22
  130.2 10.8 %collective-permute-start.4 = (bf16[2,512,512]{2,1,0:T(8,128)(2,1)}, bf16[2,512,512]{2,1,0:T(8,128)(2,1)S(1)}, u32[]{:S(2)}, u32[]{:S(2)}) collective-permute-start(bf16[2,512,512]{2,1,0:T(8,128)(2,1)} %collective-permute-done.3), channel_id=1, source_target_pairs={{0,4},{4,8},{8,12},{12,16},{16,20},{20,24},{24,28},{1,5},{5,9},{9,... | collective-permute-start | bytes 3145736 | tf_op jit(solution)/shard_map/ppermute | solution.py:34
  141.0 11.1 %fusion.37 = bf16[512,1024]{1,0:T(8,128)(2,1)S(1)} fusion(bf16[5376,1024]{1,0:T(8,128)(2,1)} %param.7, bf16[512,10752]{0,1:T(8,128)(2,1)} %copy-done.8, s32[]{:T(128)S(6)} %select_n.27), kind=kOutput, calls=%fused_computation.54 | convolution fusion | flops 5637668864 | bytes 17563652 | tf_op jit(solution)/shard_map/dot_general | solution.py:105
  152.1 1.3 copy.34
  153.4 1.4 maximum_maximum_fusion
  154.8 1.4 fusion.60
  156.2 0.4 reshape_squeeze.6
  156.6 1.0 copy.22
  157.6 2.8 reshape_squeeze.7
  160.4 17.5 %fusion.62 = (f32[4,2,512]{2,1,0:T(2,128)S(1)}, f32[4,2,512,1536]{2,3,1,0:T(8,128)}) fusion(pred[512,1536]{0,1:T(8,128)(4,1)} %fusion.22, bf16[1536,4,128,1]{0,2,3,1:T(8,128)(2,1)S(1)} %copy.22, bf16[512,4,2,128]{0,3,2,1:T(8,128)(2,1)} %bitcast.74), kind=kOutput, calls=%fused_computation.84 | convolution fusion | flops 1642071552 | bytes 28590080 | tf_op jit(solution)/shard_map/sub | solution.py:74
  177.9 12.6 %fusion.5 = f32[4,1536,128,1]{1,2,3,0:T(8,128)} fusion(bf16[512,4,2,128]{0,3,2,1:T(8,128)(2,1)} %bitcast.77, f32[4,2,512,1536]{2,3,1,0:T(8,128)} %get-tuple-element.11, f32[4,2,512]{2,1,0:T(2,128)S(1)} %get-tuple-element.10), kind=kOutput, calls=%fused_computation.10 | convolution fusion | flops 1623195648 | bytes 29376512 | tf_op jit(solution)/shard_map/kgac,akgd->ckd/dot_general | solution.py:94
  190.5 16.6 %fusion.1 = (f32[4,2,512]{2,1,0:T(2,128)S(1)}, f32[4,1536,512,2]{2,1,3,0:T(8,128)}) fusion(f32[4,2,512,1536]{2,3,1,0:T(8,128)} %get-tuple-element.11, f32[4,2,512]{2,1,0:T(2,128)S(1)} %get-tuple-element.10, bf16[512,4,2,128]{0,3,2,1:T(8,128)(2,1)S(1)} %bitcast.78, bf16[1536,4,128,1]{2,1,0,3:T(4,128)(2,1)S(1)} %bitcast.76), kind=kOutput, calls=%fused_computation.3 | convolution fusion | flops 1629483008 | bytes 52985856 | tf_op jit(solution)/shard_map/akgd,ckd->kgac/dot_general | solution.py:76
  207.1 16.8 %fusion.3 = bf16[4,2,512,1536]{2,3,1,0:T(8,128)(2,1)S(1)} fusion(f32[4,1536,512,2]{2,1,3,0:T(8,128)} %get-tuple-element.13, f32[4,2,512]{2,1,0:T(2,128)S(1)} %get-tuple-element.12, f32[4,2,512,1536]{2,3,1,0:T(8,128)} %get-tuple-element.11, f32[4,2,512]{2,1,0:T(2,128)S(1)} %get-tuple-element.10), kind=kLoop, calls=%fused_computation.5 | loop fusion | flops 25165824 | bytes 62947328 | tf_op jit(solution)/shard_map/convert_element_type | solution.py:80
  223.9 7.0 %fusion.19 = f32[4,128,1536]{2,1,0:T(8,128)} fusion(bf16[512,4,2,128]{0,3,2,1:T(8,128)(2,1)} %bitcast.75, bf16[4,2,512,1536]{2,3,1,0:T(8,128)(2,1)S(1)} %fusion.3), kind=kOutput, calls=%fused_computation.33 | convolution fusion | flops 1611399168 | bytes 16777216 | tf_op jit(solution)/shard_map/kgac,akgd->ckd/dot_general | solution.py:91
  231.0 1.8 fusion.29
  232.8 1.6 collective-permute-start.5
  234.4 5.3 collective-permute-done.5
  239.7 0.4 fusion.25
  240.0 1.3 collective-permute-start.6
  241.3 2.8 multiply_convert_fusion.1
  244.1 12.0 %collective-permute-done.6 = bf16[2,512,512]{1,2,0:T(8,128)(2,1)S(1)} collective-permute-done((bf16[2,512,512]{1,2,0:T(8,128)(2,1)S(1)}, bf16[2,512,512]{1,2,0:T(8,128)(2,1)S(1)}, u32[]{:S(2)}, u32[]{:S(2)}) %collective-permute-start.6) | collective-permute-done | bytes 1048608 | tf_op jit(solution)/shard_map/ppermute | solution.py:34
  256.1 0.4 fusion.28
  256.6 20.3 %convolution_convert_fusion = bf16[5376,2048]{1,0:T(8,128)(2,1)} fusion(bf16[512,10752]{0,1:T(8,128)(2,1)} %copy-done.8, s32[]{:T(128)S(6)} %select_n.27, bf16[512,512]{0,1:T(8,128)(2,1)S(1)} %get-tuple-element.9, bf16[512,512]{0,1:T(8,128)(2,1)S(1)} %get-tuple-element.8, bf16[512,1024]{0,1:T(8,128)(2,1)S(1)} %bitcast.79), kind=kOutput, calls=%fused_computation.8 | convolution fusion | flops 11291590656 | bytes 29622276 | tf_op jit(solution)/shard_map/dot_general | solution.py:44
  277.0 12.9 %fusion.63 = f32[512,5376]{0,1:T(8,128)} fusion(bf16[5376,1024]{1,0:T(8,128)(2,1)} %param.7, bf16[512,1024]{0,1:T(8,128)(2,1)S(1)} %bitcast.80), kind=kOutput, calls=%fused_computation.85 | convolution fusion | flops 5637144576 | bytes 23068672 | tf_op jit(solution)/shard_map/dot_general | solution.py:38
  289.9 9.4 %fusion.59 = f32[512,5376]{0,1:T(8,128)} fusion(bf16[5376,512]{1,0:T(8,128)(2,1)} %param.8, bf16[2,512,512]{1,2,0:T(8,128)(2,1)S(1)} %fusion.28), kind=kOutput, calls=%fused_computation.81 | convolution fusion | flops 2818572288 | bytes 17039360 | tf_op jit(solution)/shard_map/dot_general | solution.py:38
  299.3 19.3 %add_convert_fusion = bf16[512,5376]{0,1:T(8,128)(2,1)} fusion(f32[512,5376]{0,1:T(8,128)} %fusion.63, f32[512,5376]{0,1:T(8,128)} %fusion.59, bf16[5376,512]{1,0:T(8,128)(2,1)} %param.9, bf16[2,512,512]{1,2,0:T(8,128)(2,1)S(1)} %fusion.28), kind=kOutput, calls=%fused_computation.16 | convolution fusion | flops 2826829824 | bytes 33554432 | tf_op jit(solution)/shard_map/dot_general | solution.py:38
  318.6 110.9 %reduce-scatter.5.cloned.1.call-done = bf16[672,2048]{1,0:T(8,128)(2,1)} async-done(((bf16[5376,2048]{1,0:T(8,128)(2,1)}), bf16[672,2048]{1,0:T(8,128)(2,1)}) %reduce-scatter.5.cloned.1.call-update) | async-done | bytes 2752528 | tf_op jit(solution)/shard_map/reduce_scatter | solution.py:148
  429.5 2.4 multiply_convert_fusion
  431.9 1.2 slice.54
  433.1 1.2 fusion.61
  434.3 96.1 %reduce-scatter.3.cloned.1.call-done = bf16[512,1344]{0,1:T(8,128)(2,1)} async-done(((bf16[512,5376]{0,1:T(8,128)(2,1)}), bf16[512,1344]{0,1:T(8,128)(2,1)}) %reduce-scatter.3.cloned.1.call-update) | async-done | bytes 1376272 | tf_op jit(solution)/shard_map/reduce_scatter | solution.py:144
  (43 shorter events, 0.7 us)
Async XLA Ops:
  7.2 104.3 %copy-start.4 = (bf16[512,1344]{0,1:T(8,128)(2,1)S(1)}, bf16[512,1344]{0,1:T(8,128)(2,1)}, u32[]{:S(2)}) copy-start(bf16[512,1344]{0,1:T(8,128)(2,1)} %param.6) | copy-start | bytes 4128772
  7.2 422.3 %reduce-scatter.5.cloned.1.call-start = ((), (), s32[]{:S(2)}) async-start(), calls=%async_computation.3 | async-start | bytes 24772608 | tf_op jit(solution)/shard_map/reduce_scatter | solution.py:148
  7.2 35.5 %collective-permute-start = (bf16[512,1344]{0,1:T(8,128)(2,1)}, bf16[512,1344]{0,1:T(8,128)(2,1)S(1)}, u32[]{:S(2)}, u32[]{:S(2)}) collective-permute-start(bf16[512,1344]{0,1:T(8,128)(2,1)} %param.6), channel_id=1, source_target_pairs={{0,1},{1,2},{2,3},{3,0},{4,5},{5,6},{6,7},{7,4},{8,9},{9,10},{10,1... | collective-permute-start | bytes 4128776 | tf_op jit(solution)/shard_map/ppermute | solution.py:20
  42.7 33.3 %collective-permute-start.1 = (bf16[512,1344]{0,1:T(8,128)(2,1)S(1)}, bf16[512,1344]{0,1:T(8,128)(2,1)}, u32[]{:S(2)}, u32[]{:S(2)}) collective-permute-start(bf16[512,1344]{0,1:T(8,128)(2,1)S(1)} %collective-permute-done), channel_id=1, source_target_pairs={{0,1},{1,2},{2,3},{3,0},{4,5},{5,6},{6,7},{7,4},{8,9},{9,10},{10,1... | collective-permute-start | bytes 4128776 | tf_op jit(solution)/shard_map/ppermute | solution.py:20
  76.0 32.6 %collective-permute-start.2 = (bf16[512,1344]{0,1:T(8,128)(2,1)}, bf16[512,1344]{0,1:T(8,128)(2,1)}, u32[]{:S(2)}, u32[]{:S(2)}) collective-permute-start(bf16[512,1344]{0,1:T(8,128)(2,1)} %collective-permute-done.1), channel_id=1, source_target_pairs={{0,1},{1,2},{2,3},{3,0},{4,5},{5,6},{6,7},{7,4},{8,9},{9,10},{10,1... | collective-permute-start | bytes 4128776 | tf_op jit(solution)/shard_map/ppermute | solution.py:20
  111.5 3.5 slice-start
  113.2 2.0 slice-start.1
  114.9 5.5 %slice-start.2 = ((s8[5505024]{0:T(1024)(128)(4,1)}), s8[4194304]{0:T(1024)(128)(4,1)S(1)}, s32[]{:S(2)}) async-start(s8[5505024]{0:T(1024)(128)(4,1)} %bitcast.71), calls=%async_computation.6 | async-start | bytes 8388608
  115.2 5.2 copy-start.8
  115.2 5.5 %slice-start.3 = ((s8[5505024]{0:T(1024)(128)(4,1)}), s8[1310720]{0:T(1024)(128)(4,1)S(1)}, s32[]{:S(2)}) async-start(s8[5505024]{0:T(1024)(128)(4,1)} %bitcast.71), calls=%async_computation.7 | async-start | bytes 2621440
  120.7 5.5 %copy-start.5 = (bf16[512,1024]{1,0:T(8,128)(2,1)S(1)}, bf16[512,1024]{1,0:T(8,128)(2,1)}, u32[]{:S(2)}) copy-start(bf16[512,1024]{1,0:T(8,128)(2,1)} %param.10) | copy-start | bytes 3145732
  120.7 6.8 %copy-start.9 = (s32[4096]{0:T(1024)S(1)}, s32[4096]{0:T(1024)}, u32[]{:S(2)}) copy-start(s32[4096]{0:T(1024)} %param.11) | copy-start | bytes 49156
  123.8 6.4 %collective-permute-start.3 = (bf16[2,512,512]{2,1,0:T(8,128)(2,1)S(1)}, bf16[2,512,512]{2,1,0:T(8,128)(2,1)}, u32[]{:S(2)}, u32[]{:S(2)}) collective-permute-start(bf16[2,512,512]{2,1,0:T(8,128)(2,1)S(1)} %pad_maximum_fusion.1), channel_id=1, source_target_pairs={{0,4},{4,8},{8,12},{12,16},{16,20},{20,24},{24,28},{1,5},{5,9},{9,... | collective-permute-start | bytes 3145736 | tf_op jit(solution)/shard_map/ppermute | solution.py:34
  130.2 23.2 %collective-permute-start.4 = (bf16[2,512,512]{2,1,0:T(8,128)(2,1)}, bf16[2,512,512]{2,1,0:T(8,128)(2,1)S(1)}, u32[]{:S(2)}, u32[]{:S(2)}) collective-permute-start(bf16[2,512,512]{2,1,0:T(8,128)(2,1)} %collective-permute-done.3), channel_id=1, source_target_pairs={{0,4},{4,8},{8,12},{12,16},{16,20},{20,24},{24,28},{1,5},{5,9},{9,... | collective-permute-start | bytes 3145736 | tf_op jit(solution)/shard_map/ppermute | solution.py:34
  157.6 20.3 %copy-start.2 = (bf16[1536,4,128,1]{0,2,3,1:T(8,128)(2,1)}, bf16[1536,4,128,1]{0,2,3,1:T(8,128)(2,1)S(1)}, u32[]{:S(2)}) copy-start(bf16[1536,4,128,1]{0,2,3,1:T(8,128)(2,1)S(1)} %copy.22) | copy-start | bytes 4718596
  177.9 12.6 %copy-start.6 = (bf16[512,1024]{0,1:T(8,128)(2,1)S(1)}, bf16[512,1024]{0,1:T(8,128)(2,1)}, u32[]{:S(2)}) copy-start(bf16[512,1024]{0,1:T(8,128)(2,1)} %copy.35) | copy-start | bytes 3145732
  231.0 8.7 %copy-start = (f32[4,128,1536]{2,1,0:T(8,128)S(1)}, f32[4,128,1536]{2,1,0:T(8,128)}, u32[]{:S(2)}) copy-start(f32[4,128,1536]{2,1,0:T(8,128)} %fusion.19) | copy-start | bytes 9437188
  231.0 8.7 %copy-start.1 = (f32[4,1536,128,1]{1,2,3,0:T(8,128)S(1)}, f32[4,1536,128,1]{1,2,3,0:T(8,128)}, u32[]{:S(2)}) copy-start(f32[4,1536,128,1]{1,2,3,0:T(8,128)} %fusion.5) | copy-start | bytes 9437188
  232.8 8.5 %copy-start.3 = (bf16[1536,4,128,1]{0,2,3,1:T(8,128)(2,1)S(1)}, bf16[1536,4,128,1]{0,2,3,1:T(8,128)(2,1)}, u32[]{:S(2)}) copy-start(bf16[1536,4,128,1]{0,2,3,1:T(8,128)(2,1)} %copy-done.2) | copy-start | bytes 4718596
  232.8 6.8 %collective-permute-start.5 = (bf16[2,512,512]{1,2,0:T(8,128)(2,1)S(1)}, bf16[2,512,512]{1,2,0:T(8,128)(2,1)S(1)}, u32[]{:S(2)}, u32[]{:S(2)}) collective-permute-start(bf16[2,512,512]{1,2,0:T(8,128)(2,1)S(1)} %fusion.29), channel_id=1, source_target_pairs={{4,0},{8,4},{12,8},{16,12},{20,16},{24,20},{28,24},{5,1},{9,5},{13... | collective-permute-start | bytes 3145736 | tf_op jit(solution)/shard_map/ppermute | solution.py:34
  240.0 16.1 %collective-permute-start.6 = (bf16[2,512,512]{1,2,0:T(8,128)(2,1)S(1)}, bf16[2,512,512]{1,2,0:T(8,128)(2,1)S(1)}, u32[]{:S(2)}, u32[]{:S(2)}) collective-permute-start(bf16[2,512,512]{1,2,0:T(8,128)(2,1)S(1)} %fusion.25), channel_id=1, source_target_pairs={{4,0},{8,4},{12,8},{16,12},{20,16},{24,20},{28,24},{5,1},{9,5},{13... | collective-permute-start | bytes 3145736 | tf_op jit(solution)/shard_map/ppermute | solution.py:34
  244.1 12.5 %copy-start.7 = (bf16[4,128,2,512]{3,1,2,0:T(8,128)(2,1)S(1)}, bf16[4,128,2,512]{3,1,2,0:T(8,128)(2,1)}, u32[]{:S(2)}) copy-start(bf16[4,128,2,512]{3,1,2,0:T(8,128)(2,1)} %multiply_convert_fusion.1) | copy-start | bytes 3145732
  276.9 253.4 %reduce-scatter.3.cloned.1.call-start = ((), (), s32[]{:S(2)}) async-start(), calls=%async_computation.2 | async-start | bytes 6881280 | tf_op jit(solution)/shard_map/reduce_scatter | solution.py:144
Sparse Core Ops, SparseCore 0:
  277.1 152.3 reduce-scatter.4
  432.3 97.9 reduce-scatter.2
